TPU v7x, 512 devices: a whole 4x4x16 slice. The times are simulated.
512 devices in a mesh: pos: 64 (over z, y), mode: 8 (over x, core).
Axes of the slice: x: 4, y: 4, z: 16, core: 2. Of those that a mesh axis runs over, the one named last changes fastest.
Arguments:
- object_field: float32 [2, 8192, 512], P(None, 'pos'), may hold values from -6 to 6
- probe: float32 [2, 8, 256, 256], P(None, 'mode'), may hold values from -3 to 3
- measured: float32 [192, 256, 256], P('pos'), may hold values from 0 to 16
- row_offsets: int32 [192], P('pos'), may hold values from 0 to 127
- col_offsets: int32 [192], P('pos'), may hold values from 0 to 256
- tile_counts: int32 [64], P('pos'), may hold values from 1 to 3, 96 in all
Outputs:
- updated_object: float32 [2, 8192, 512], P(None, ('pos', 'mode'))
Inputs may be any that keep to these rules, and one draw needn't show every extreme that they name: Slots 0 to tile_counts[t] - 1 of tile t hold scan positions, the others are empty; the counts sum to 96 and the largest equals 3.
All inputs are finite; a program needn't handle non-finite values. No bound on the sum of `tile_counts` on one device may be relied on, other than what follows from the above.
Results may differ from a plain program's by a relative error of at most 0.0016.
Values sent between devices are 32-bit elements; how exact they have to be, the bound alone decides.
No kernel may reach another device: no remote copies, remote signals or barrier semaphores. Data moves between devices by JAX's collectives and lax.ppermute only.
A program may use at most 64 MiB of HBM per device.

v0:
```python
import math

import jax
import jax.numpy as jnp
from jax import lax
from jax.experimental import pallas as pl
from jax.experimental.pallas import tpu as pltpu
from jax.sharding import PartitionSpec as P


def dft_tables(pattern):
    counter = jnp.arange(pattern, dtype=jnp.int32)
    phases = counter[:, None] * counter[None, :] % pattern
    angles = phases.astype(jnp.float32) * (2.0 * math.pi / pattern)
    factor = 1.0 / math.sqrt(pattern)
    return (
        (jnp.cos(angles) * factor).astype(jnp.bfloat16),
        (-jnp.sin(angles) * factor).astype(jnp.bfloat16),
    )


def neighbour_pairs(size, step):
    if step > 0:
        return [(i, i + 1) for i in range(size - 1)]
    return [(i + 1, i) for i in range(size - 1)]


def mode_pairs():
    n = lax.axis_size("mode")
    chips = n // 2
    core = [(i, i ^ 1) for i in range(n)]
    near = [(i, i ^ 2) for i in range(n)]
    far = [(i, 2 * (chips - 1 - i // 2) + i % 2) for i in range(n)]
    return core, near, far


def allreduce_chips(qa, qb):
    _, near, far = mode_pairs()
    qa = qa + lax.ppermute(qa, "mode", near)
    qb = qb + lax.ppermute(qb, "mode", far)
    return (qa, lax.ppermute(qa, "mode", far)), (qb, lax.ppermute(qb, "mode", near))


def reduce_scatter_mode(x):
    core_pairs, near, far = mode_pairs()
    n = lax.axis_size("mode")
    m = lax.axis_index("mode")
    c, rows, w = x.shape
    x = x.reshape(c, 2, 2, 2, rows // n, w)
    for pairs, dim, d in ((core_pairs, 3, 1), (far, 1, 4), (near, 1, 2)):
        bit = (m // d) % 2
        keep = lax.dynamic_index_in_dim(x, bit, axis=dim, keepdims=False)
        send = lax.dynamic_index_in_dim(x, 1 - bit, axis=dim, keepdims=False)
        x = keep + lax.ppermute(send, "mode", pairs)
    return x.reshape(c, rows // n, w)


def _dot(a, b):
    return jnp.dot(a, b, preferred_element_type=jnp.float32)


def _window(ext_ref, k, r, c, pat):
    width = ext_ref.shape[2]
    base = pl.multiple_of((r // 8) * 8, 8)
    span = pat + 8
    down = (span - (r - base)) % span
    rows = pltpu.roll(ext_ref[k, pl.ds(base, span), :], down, 0)[:pat]
    return pltpu.roll(rows, (width - c) % width, 1)[:, :pat]


def _place(ref, a, r, c):
    pat = a.shape[0]
    width = ref.shape[-1]
    base = pl.multiple_of((r // 8) * 8, 8)
    span = pat + 8
    wide = pltpu.roll(jnp.concatenate([a, jnp.zeros((pat, width - pat), jnp.float32)], axis=1), c, 1)
    tall = jnp.concatenate([wide, jnp.zeros((span - pat, width), jnp.float32)], axis=0)
    ref[pl.ds(base, span), :] += pltpu.roll(tall, r - base, 0)


def forward_kernel(roff, coff, cnt, core, before_ref, own_ref, after_ref, pa_ref, pb_ref, fr_ref, fi_ref,
                   exit_ref, wave_ref, power_a_ref, power_b_ref, ext_ref):
    i = pl.program_id(0)
    slots = roff.shape[0]
    pat = pa_ref.shape[1]
    band = own_ref.shape[1]
    g = core[0] + 2 * i
    gi = jnp.minimum(g, slots - 1)
    live = g < cnt[0]

    def store_power(value):
        @pl.when(i == 0)
        def _():
            power_a_ref[...] = value

        @pl.when(i == 1)
        def _():
            power_b_ref[...] = value

    @pl.when(jnp.logical_and(i == 0, core[0] == 0))
    def _():
        ext_ref[:, :band, :] = before_ref[...]
        ext_ref[:, band : 2 * band, :] = own_ref[...]
        ext_ref[:, 2 * band :, :] = after_ref[...]

    @pl.when(jnp.logical_and(i == 0, core[0] == 1))
    def _():
        ext_ref[:, :band, :] = after_ref[...]
        ext_ref[:, band : 2 * band, :] = own_ref[...]
        ext_ref[:, 2 * band :, :] = before_ref[...]

    @pl.when(live)
    def _():
        r = roff[gi]
        c = coff[gi]
        obj_re = _window(ext_ref, 0, r, c, pat)
        obj_im = _window(ext_ref, 1, r, c, pat)
        fr = fr_ref[...]
        fi = fi_ref[...]
        total = None
        for k, p_ref in enumerate((pa_ref, pb_ref)):
            p_re = p_ref[0]
            p_im = p_ref[1]
            e_re = (p_re * obj_re - p_im * obj_im).astype(jnp.bfloat16)
            e_im = (p_re * obj_im + p_im * obj_re).astype(jnp.bfloat16)
            h_re = (_dot(fr, e_re) - _dot(fi, e_im)).astype(jnp.bfloat16)
            h_im = (_dot(fr, e_im) + _dot(fi, e_re)).astype(jnp.bfloat16)
            v_re = _dot(h_re, fr) - _dot(h_im, fi)
            v_im = _dot(h_re, fi) + _dot(h_im, fr)
            exit_ref[0, k, 0] = e_re
            exit_ref[0, k, 1] = e_im
            wave_ref[0, k, 0] = h_re
            wave_ref[0, k, 1] = h_im
            part = v_re * v_re + v_im * v_im
            total = part if total is None else total + part
        store_power(total)

    @pl.when(g == slots)
    def _():
        total = None
        for p_ref in (pa_ref, pb_ref):
            p_re = p_ref[0]
            p_im = p_ref[1]
            part = p_re * p_re + p_im * p_im
            total = part if total is None else total + part
        store_power(total)

    @pl.when(jnp.logical_and(jnp.logical_not(live), g != slots))
    def _():
        store_power(jnp.zeros((pat, pat), jnp.float32))


def backward_kernel(roff, coff, cnt, core, exit_ref, wave_ref, ma_ref, ra_ref, mb_ref, rb_ref, meas_ref,
                    pa_ref, pb_ref, fr_ref, fi_ref, keep_ref, message_ref, own_illum_ref, numer_ref, illum_ref):
    i = pl.program_id(0)
    last = pl.num_programs(0) - 1
    slots = roff.shape[0]
    g = core[0] + 2 * i
    gi = jnp.minimum(g, slots - 1)

    @pl.when(i == 0)
    def _():
        numer_ref[...] = jnp.zeros(numer_ref.shape, jnp.float32)
        illum_ref[...] = jnp.zeros(illum_ref.shape, jnp.float32)

    @pl.when(g < cnt[0])
    def _():
        r = roff[gi]
        c = coff[gi]
        model = jnp.where(i == 0, ma_ref[...] + ra_ref[...], mb_ref[...] + rb_ref[...])
        scaling = jnp.sqrt(meas_ref[0]) / jnp.maximum(jnp.sqrt(model), 1.0)
        fr = fr_ref[...]
        fi = fi_ref[...]
        n_re = None
        n_im = None
        for k, p_ref in enumerate((pa_ref, pb_ref)):
            h_re = wave_ref[0, k, 0]
            h_im = wave_ref[0, k, 1]
            v_re = _dot(h_re, fr) - _dot(h_im, fi)
            v_im = _dot(h_re, fi) + _dot(h_im, fr)
            x_re = (scaling * v_re).astype(jnp.bfloat16)
            x_im = (scaling * v_im).astype(jnp.bfloat16)
            b_re = (_dot(fr, x_re) + _dot(fi, x_im)).astype(jnp.bfloat16)
            b_im = (_dot(fr, x_im) - _dot(fi, x_re)).astype(jnp.bfloat16)
            d_re = _dot(b_re, fr) + _dot(b_im, fi) - exit_ref[0, k, 0].astype(jnp.float32)
            d_im = _dot(b_im, fr) - _dot(b_re, fi) - exit_ref[0, k, 1].astype(jnp.float32)
            p_re = p_ref[0]
            p_im = p_ref[1]
            t_re = p_re * d_re + p_im * d_im
            t_im = p_re * d_im - p_im * d_re
            n_re = t_re if n_re is None else n_re + t_re
            n_im = t_im if n_im is None else n_im + t_im
        _place(numer_ref.at[0], n_re, r, c)
        _place(numer_ref.at[1], n_im, r, c)

    @pl.when(jnp.logical_and(core[0] == 1, i == last))
    def _():
        for slot in range(slots):
            @pl.when(slot < cnt[0])
            def _():
                _place(illum_ref, mb_ref[...] + rb_ref[...], roff[slot], coff[slot])

    @pl.when(i == last)
    def _():
        side = core[0]
        mode = core[1]
        partner = mode + 1 - 2 * side
        band = numer_ref.shape[1] // 3
        share = band // 8
        quads = 4
        for ch in range(2):
            for b in range(3):
                for q in range(quads):
                    dst = ((ch * 3 + b) * quads + q) * share
                    kept = pl.multiple_of(b * band + (2 * q + side) * share, 8)
                    sent = pl.multiple_of(b * band + (2 * q + 1 - side) * share, 8)
                    keep_ref[dst : dst + share, :] = numer_ref[ch, pl.ds(kept, share), :]
                    message_ref[dst : dst + share, :] = numer_ref[ch, pl.ds(sent, share), :]
        top = 2 * 3 * quads * share
        for b in range(3):
            theirs = pl.multiple_of(b * band + partner * share, 8)
            mine = pl.multiple_of(b * band + mode * share, 8)
            message_ref[top + b * share : top + (b + 1) * share, :] = illum_ref[pl.ds(theirs, share), :]
            own_illum_ref[b * share : (b + 1) * share, :] = illum_ref[pl.ds(mine, share), :]


def run_forward(before, own, after, pa, pb, fr, fi, roff, coff, cnt, core):
    slots = roff.shape[0]
    local = (slots + 1) // 2
    pat = pa.shape[1]
    whole3 = lambda i, *_: (0, 0, 0)
    whole2 = lambda i, *_: (0, 0)
    per5 = lambda i, *_: (i, 0, 0, 0, 0)
    flops = local * 2 * 8 * 2 * pat ** 3
    ext_shape = (2, 3 * own.shape[1], own.shape[2])
    return pl.pallas_call(
        forward_kernel,
        grid_spec=pltpu.PrefetchScalarGridSpec(
            num_scalar_prefetch=4,
            grid=(local,),
            in_specs=[
                pl.BlockSpec(before.shape, whole3),
                pl.BlockSpec(own.shape, whole3),
                pl.BlockSpec(after.shape, whole3),
                pl.BlockSpec(pa.shape, whole3),
                pl.BlockSpec(pb.shape, whole3),
                pl.BlockSpec(fr.shape, whole2),
                pl.BlockSpec(fi.shape, whole2),
            ],
            out_specs=[
                pl.BlockSpec((1, 2, 2, pat, pat), per5),
                pl.BlockSpec((1, 2, 2, pat, pat), per5),
                pl.BlockSpec((pat, pat), whole2),
                pl.BlockSpec((pat, pat), whole2),
            ],
            scratch_shapes=[pltpu.VMEM(ext_shape, jnp.float32)],
        ),
        out_shape=[
            jax.ShapeDtypeStruct((local, 2, 2, pat, pat), jnp.bfloat16),
            jax.ShapeDtypeStruct((local, 2, 2, pat, pat), jnp.bfloat16),
            jax.ShapeDtypeStruct((pat, pat), jnp.float32),
            jax.ShapeDtypeStruct((pat, pat), jnp.float32),
        ],
        compiler_params=pltpu.CompilerParams(dimension_semantics=("arbitrary",)),
        cost_estimate=pl.CostEstimate(flops=flops, transcendentals=0, bytes_accessed=10 * 1024 * 1024),
    )(roff, coff, cnt, core, before, own, after, pa, pb, fr, fi)


def run_backward(exits, waves, model_a, model_b, measured, pa, pb, fr, fi, roff, coff, cnt, ids,
                 ext_rows, width):
    slots = roff.shape[0]
    local = (slots + 1) // 2
    pat = pa.shape[1]
    share = ext_rows // 3 // 8
    kept_rows = 2 * ext_rows // 2
    whole3 = lambda i, *_: (0, 0, 0)
    whole2 = lambda i, *_: (0, 0)
    per5 = lambda i, *_: (i, 0, 0, 0, 0)
    slot_of = lambda i, roff, coff, cnt, core: (jnp.minimum(core[0] + 2 * i, slots - 1), 0, 0)
    flops = local * 2 * 8 * 2 * pat ** 3
    return pl.pallas_call(
        backward_kernel,
        grid_spec=pltpu.PrefetchScalarGridSpec(
            num_scalar_prefetch=4,
            grid=(local,),
            in_specs=[
                pl.BlockSpec((1, 2, 2, pat, pat), per5),
                pl.BlockSpec((1, 2, 2, pat, pat), per5),
                pl.BlockSpec((pat, pat), whole2),
                pl.BlockSpec((pat, pat), whole2),
                pl.BlockSpec((pat, pat), whole2),
                pl.BlockSpec((pat, pat), whole2),
                pl.BlockSpec((1, pat, pat), slot_of),
                pl.BlockSpec(pa.shape, whole3),
                pl.BlockSpec(pb.shape, whole3),
                pl.BlockSpec(fr.shape, whole2),
                pl.BlockSpec(fi.shape, whole2),
            ],
            out_specs=[
                pl.BlockSpec((kept_rows, width), whole2),
                pl.BlockSpec((kept_rows + 3 * share, width), whole2),
                pl.BlockSpec((3 * share, width), whole2),
            ],
            scratch_shapes=[
                pltpu.VMEM((2, ext_rows, width), jnp.float32),
                pltpu.VMEM((ext_rows, width), jnp.float32),
            ],
        ),
        out_shape=[
            jax.ShapeDtypeStruct((kept_rows, width), jnp.float32),
            jax.ShapeDtypeStruct((kept_rows + 3 * share, width), jnp.float32),
            jax.ShapeDtypeStruct((3 * share, width), jnp.float32),
        ],
        compiler_params=pltpu.CompilerParams(dimension_semantics=("arbitrary",)),
        cost_estimate=pl.CostEstimate(flops=flops, transcendentals=0, bytes_accessed=12 * 1024 * 1024),
    )(roff, coff, cnt, ids, exits, waves, *model_a, *model_b, measured, pa, pb, fr, fi)


def local(object_field, probe, measured, row_offsets, col_offsets, tile_counts):
    rows_tile = object_field.shape[1]
    width = object_field.shape[2]
    pos_count = lax.axis_size("pos")
    mode_count = lax.axis_size("mode")
    my_mode = lax.axis_index("mode")
    share_rows = rows_tile // mode_count
    pattern = probe.shape[2]
    fr, fi = dft_tables(pattern)
    probe2 = probe[:, 0]

    core_pairs, near, far = mode_pairs()
    core = my_mode % 2
    halo_pairs = []
    for p in range(pos_count):
        for m in range(mode_count):
            if m % 2 == 0 and p + 1 < pos_count:
                halo_pairs.append((p * mode_count + m, (p + 1) * mode_count + m))
            if m % 2 == 1 and p >= 1:
                halo_pairs.append((p * mode_count + m, (p - 1) * mode_count + m))
    fetched = lax.ppermute(object_field, ("pos", "mode"), halo_pairs)
    partner_probe = lax.ppermute(probe2, "mode", core_pairs)
    swapped = lax.ppermute(fetched, "mode", core_pairs)
    ext_rows = 3 * rows_tile

    roff = row_offsets.astype(jnp.int32)
    coff = col_offsets.astype(jnp.int32)
    cnt = tile_counts.astype(jnp.int32)
    ids = jnp.stack([core, my_mode]).astype(jnp.int32)

    exits, waves, power_a, power_b = run_forward(
        fetched, object_field, swapped, probe2, partner_probe, fr, fi, roff, coff, cnt, ids
    )
    model_a, model_b = allreduce_chips(power_a, power_b)
    kept, message, own_illum = run_backward(
        exits, waves, model_a, model_b, measured, probe2, partner_probe, fr, fi, roff, coff, cnt, ids,
        ext_rows, width
    )

    got = lax.ppermute(message, "mode", core_pairs)
    numer_rows = kept.shape[0]
    block_shape = (2, 3, 2, 2, share_rows, width)
    blocks = kept.reshape(block_shape) + got[:numer_rows].reshape(block_shape)
    own_illum = own_illum.reshape(3, share_rows, width) + got[numer_rows:].reshape(3, share_rows, width)
    band_rows = 2 * 4 * share_rows
    to_next = jnp.concatenate([blocks[:, 2].reshape(band_rows, width), own_illum[2]], axis=0)
    to_prev = jnp.concatenate([blocks[:, 0].reshape(band_rows, width), own_illum[0]], axis=0)
    from_prev = lax.ppermute(to_next, "pos", neighbour_pairs(pos_count, 1))
    from_next = lax.ppermute(to_prev, "pos", neighbour_pairs(pos_count, -1))
    tile = (
        blocks[:, 1]
        + from_prev[:band_rows].reshape(blocks[:, 1].shape)
        + from_next[:band_rows].reshape(blocks[:, 1].shape)
    )
    illum_rows = own_illum[1] + from_prev[band_rows:] + from_next[band_rows:]
    for pairs, d in ((far, 4), (near, 2)):
        bit = (my_mode // d) % 2
        keep = lax.dynamic_index_in_dim(tile, bit, axis=1, keepdims=False)
        send = lax.dynamic_index_in_dim(tile, 1 - bit, axis=1, keepdims=False)
        tile = keep + lax.ppermute(send, "mode", pairs)

    start = my_mode * share_rows
    own_rows = lax.dynamic_slice_in_dim(object_field, start, share_rows, 1)
    return own_rows + tile / (illum_rows + 1.0)


def solution(mesh):
    in_specs = (
        P(None, "pos", None),
        P(None, "mode", None, None),
        P("pos", None, None),
        P("pos"),
        P("pos"),
        P("pos"),
    )
    out_specs = P(None, ("pos", "mode"), None)
    return jax.shard_map(local, mesh=mesh, in_specs=in_specs, out_specs=out_specs, check_vma=False)
```

profile of v0, /device:TPU:248, one launch (start us, length us, event | category | flops | bytes accessed | tf_op | source)
XLA Modules:
  0.0 102.2 jit_solution(7286414678089867299)
XLA Ops:
  0.0 4.7 %collective-permute-start = (f32[2,128,512]{2,1,0:T(8,128)}, f32[2,128,512]{2,1,0:T(8,128)S(1)}, u32[]{:S(2)}, u32[]{:S(2)}) collective-permute-start(f32[2,128,512]{2,1,0:T(8,128)} %own_ref.1), channel_id=1, source_target_pairs={{0,8},{2,10},{4,12},{6,14},{8,16},{9,1},{10,18},{11,3},{12,20},{13... | collective-permute-start | bytes 1572872 | tf_op jit(solution)/shard_map/ppermute | solution.py:339
  4.7 1.9 %collective-permute-start.2 = (f32[2,256,256]{2,1,0:T(8,128)}, f32[2,256,256]{2,1,0:T(8,128)S(1)}, u32[]{:S(2)}, u32[]{:S(2)}) collective-permute-start(f32[2,256,256]{2,1,0:T(8,128)} %bitcast.35), channel_id=1, source_target_pairs={{0,1},{1,0},{2,3},{3,2},{4,5},{5,4},{6,7},{7,6},{8,9},{9,8},{10,11... | collective-permute-start | bytes 1572872 | tf_op jit(solution)/shard_map/ppermute | solution.py:340
  6.6 5.1 %collective-permute-done.before_ref = f32[2,128,512]{2,1,0:T(8,128)S(1)} collective-permute-done((f32[2,128,512]{2,1,0:T(8,128)}, f32[2,128,512]{2,1,0:T(8,128)S(1)}, u32[]{:S(2)}, u32[]{:S(2)}) %collective-permute-start) | collective-permute-done | bytes 524320 | tf_op jit(solution)/shard_map/ppermute | solution.py:339
  11.7 3.5 %collective-permute-start.1 = (f32[2,128,512]{2,1,0:T(8,128)S(1)}, f32[2,128,512]{2,1,0:T(8,128)S(1)}, u32[]{:S(2)}, u32[]{:S(2)}) collective-permute-start(f32[2,128,512]{2,1,0:T(8,128)S(1)} %collective-permute-done.before_ref), channel_id=1, source_target_pairs={{0,1},{1,0},{2,3},{3,2},{4,5},{5,4},{6,7},{7,6},{8,9},{9,8},{10,11... | collective-permute-start | bytes 1572872 | tf_op jit(solution)/shard_map/ppermute | solution.py:341
  16.4 1.8 %multiply_convert_fusion = (bf16[256,256]{1,0:T(8,128)(2,1)}, bf16[256,256]{1,0:T(8,128)(2,1)}) fusion(), kind=kLoop, calls=%fused_computation.12 | loop fusion | flops 1245184 | bytes 262144 | tf_op jit(solution)/shard_map/convert_element_type | solution.py:18
  19.2 5.6 %shard_map.64 = (bf16[2,2,2,256,256]{4,3,2,1,0:T(8,128)(2,1)}, bf16[2,2,2,256,256]{4,3,2,1,0:T(8,128)(2,1)}, f32[256,256]{1,0:T(8,128)}, f32[256,256]{1,0:T(8,128)}) custom-call(s32[3]{0:T(128)} %roff.3, s32[3]{0:T(128)} %coff.3, s32[1]{0:T(128)S(6)} %copy.25.cnt, s32[2]{0:T(128)} %pad_add_fusion.core, f32[2,128,512]{2,1,0:T(8,128)} %copy-done.8, ...), custom_call_target="tpu_custom_call" | custom-call | flops 1073741824 | bytes 10485760 | tf_op jit(solution)/shard_map/pallas_call | solution.py:236
  24.8 4.7 %collective-permute-start.5 = (f32[256,256]{1,0:T(8,128)}, f32[256,256]{1,0:T(8,128)S(1)}, u32[]{:S(2)}, u32[]{:S(2)}) collective-permute-start(f32[256,256]{1,0:T(8,128)} %get-tuple-element.15), channel_id=1, source_target_pairs={{0,6},{1,7},{2,4},{3,5},{4,2},{5,3},{6,0},{7,1},{8,14},{9,15},{10,... | collective-permute-start | bytes 786440 | tf_op jit(solution)/shard_map/ppermute | solution.py:40
  29.5 2.3 %collective-permute-start.3 = (f32[256,256]{1,0:T(8,128)}, f32[256,256]{1,0:T(8,128)S(1)}, u32[]{:S(2)}, u32[]{:S(2)}) collective-permute-start(f32[256,256]{1,0:T(8,128)} %get-tuple-element.14), channel_id=1, source_target_pairs={{0,2},{1,3},{2,0},{3,1},{4,6},{5,7},{6,4},{7,5},{8,10},{9,11},{10,... | collective-permute-start | bytes 786440 | tf_op jit(solution)/shard_map/ppermute | solution.py:39
  31.8 3.1 %collective-permute-done.5 = f32[256,256]{1,0:T(8,128)S(1)} collective-permute-done((f32[256,256]{1,0:T(8,128)}, f32[256,256]{1,0:T(8,128)S(1)}, u32[]{:S(2)}, u32[]{:S(2)}) %collective-permute-start.5) | collective-permute-done | bytes 262176 | tf_op jit(solution)/shard_map/ppermute | solution.py:40
  35.9 2.2 %collective-permute-start.6 = (f32[256,256]{1,0:T(8,128)S(1)}, f32[256,256]{1,0:T(8,128)S(1)}, u32[]{:S(2)}, u32[]{:S(2)}) collective-permute-start(f32[256,256]{1,0:T(8,128)S(1)} %add.90.mb_ref), channel_id=1, source_target_pairs={{0,2},{1,3},{2,0},{3,1},{4,6},{5,7},{6,4},{7,5},{8,10},{9,11},{10,... | collective-permute-start | bytes 786440 | tf_op jit(solution)/shard_map/ppermute | solution.py:41
  38.4 4.1 %collective-permute-start.4 = (f32[256,256]{1,0:T(8,128)S(1)}, f32[256,256]{1,0:T(8,128)S(1)}, u32[]{:S(2)}, u32[]{:S(2)}) collective-permute-start(f32[256,256]{1,0:T(8,128)S(1)} %add.89.ma_ref), channel_id=1, source_target_pairs={{0,6},{1,7},{2,4},{3,5},{4,2},{5,3},{6,0},{7,1},{8,14},{9,15},{10,... | collective-permute-start | bytes 786440 | tf_op jit(solution)/shard_map/ppermute | solution.py:41
  42.6 1.6 %collective-permute-done.6.rb_ref = f32[256,256]{1,0:T(8,128)S(1)} collective-permute-done((f32[256,256]{1,0:T(8,128)S(1)}, f32[256,256]{1,0:T(8,128)S(1)}, u32[]{:S(2)}, u32[]{:S(2)}) %collective-permute-start.6) | collective-permute-done | bytes 262176 | tf_op jit(solution)/shard_map/ppermute | solution.py:41
  44.1 3.7 %collective-permute-done.4.ra_ref = f32[256,256]{1,0:T(8,128)S(1)} collective-permute-done((f32[256,256]{1,0:T(8,128)S(1)}, f32[256,256]{1,0:T(8,128)S(1)}, u32[]{:S(2)}, u32[]{:S(2)}) %collective-permute-start.4) | collective-permute-done | bytes 262176 | tf_op jit(solution)/shard_map/ppermute | solution.py:41
  48.6 6.8 %shard_map.65 = (f32[384,512]{1,0:T(8,128)}, f32[432,512]{1,0:T(8,128)}, f32[48,512]{1,0:T(8,128)}) custom-call(s32[3]{0:T(128)} %roff.3, s32[3]{0:T(128)} %coff.3, s32[1]{0:T(128)S(6)} %copy.25.cnt, s32[2]{0:T(128)} %pad_add_fusion.core, bf16[2,2,2,256,256]{4,3,2,1,0:T(8,128)(2,1)} %get-tuple-element.12.exit_ref, ...), custom_call_target="tpu_custom_call" | custom-call | flops 1073741824 | bytes 12582912 | tf_op jit(solution)/shard_map/pallas_call | solution.py:281
  55.4 1.9 %collective-permute-start.7 = (f32[432,512]{1,0:T(8,128)}, f32[432,512]{1,0:T(8,128)S(1)}, u32[]{:S(2)}, u32[]{:S(2)}) collective-permute-start(f32[432,512]{1,0:T(8,128)} %get-tuple-element.17), channel_id=1, source_target_pairs={{0,1},{1,0},{2,3},{3,2},{4,5},{5,4},{6,7},{7,6},{8,9},{9,8},{10,11... | collective-permute-start | bytes 2654216 | tf_op jit(solution)/shard_map/ppermute | solution.py:358
  57.3 2.6 %collective-permute-done.7 = f32[432,512]{1,0:T(8,128)S(1)} collective-permute-done((f32[432,512]{1,0:T(8,128)}, f32[432,512]{1,0:T(8,128)S(1)}, u32[]{:S(2)}, u32[]{:S(2)}) %collective-permute-start.7) | collective-permute-done | bytes 884768 | tf_op jit(solution)/shard_map/ppermute | solution.py:358
  62.2 9.1 %collective-permute-start.8 = (f32[144,512]{1,0:T(8,128)S(1)}, f32[144,512]{1,0:T(8,128)S(1)}, u32[]{:S(2)}, u32[]{:S(2)}) collective-permute-start(f32[144,512]{1,0:T(8,128)S(1)} %pad_maximum_fusion), channel_id=1, source_target_pairs={{0,8},{8,16},{16,24},{24,32},{32,40},{40,48},{48,56},{56,64},{64,7... | collective-permute-start | bytes 884744 | tf_op jit(solution)/shard_map/ppermute | solution.py:366
  71.3 1.9 %collective-permute-start.9 = (f32[144,512]{1,0:T(8,128)S(1)}, f32[144,512]{1,0:T(8,128)S(1)}, u32[]{:S(2)}, u32[]{:S(2)}) collective-permute-start(f32[144,512]{1,0:T(8,128)S(1)} %pad_maximum_fusion.1), channel_id=1, source_target_pairs={{8,0},{16,8},{24,16},{32,24},{40,32},{48,40},{56,48},{64,56},{72,6... | collective-permute-start | bytes 884744 | tf_op jit(solution)/shard_map/ppermute | solution.py:367
  73.3 4.6 %collective-permute-done.8 = f32[144,512]{1,0:T(8,128)S(1)} collective-permute-done((f32[144,512]{1,0:T(8,128)S(1)}, f32[144,512]{1,0:T(8,128)S(1)}, u32[]{:S(2)}, u32[]{:S(2)}) %collective-permute-start.8) | collective-permute-done | bytes 294944 | tf_op jit(solution)/shard_map/ppermute | solution.py:366
  78.5 6.7 %collective-permute-done.9 = f32[144,512]{1,0:T(8,128)S(1)} collective-permute-done((f32[144,512]{1,0:T(8,128)S(1)}, f32[144,512]{1,0:T(8,128)S(1)}, u32[]{:S(2)}, u32[]{:S(2)}) %collective-permute-start.9) | collective-permute-done | bytes 294944 | tf_op jit(solution)/shard_map/ppermute | solution.py:367
  86.3 4.7 %collective-permute-start.10 = (f32[2,2,16,512]{3,2,1,0:T(8,128)S(1)}, f32[2,2,16,512]{3,2,1,0:T(8,128)S(1)}, u32[]{:S(2)}, u32[]{:S(2)}) collective-permute-start(f32[2,2,16,512]{3,2,1,0:T(8,128)S(1)} %dynamic-slice_bitcast_fusion), channel_id=1, source_target_pairs={{0,6},{1,7},{2,4},{3,5},{4,2},{5,3},{6,0},{7,1},{8,14},{9,15},{10,... | collective-permute-start | bytes 393224 | tf_op jit(solution)/shard_map/ppermute | solution.py:378
  91.1 3.4 %collective-permute-done.10 = f32[2,2,16,512]{3,2,1,0:T(8,128)S(1)} collective-permute-done((f32[2,2,16,512]{3,2,1,0:T(8,128)S(1)}, f32[2,2,16,512]{3,2,1,0:T(8,128)S(1)}, u32[]{:S(2)}, u32[]{:S(2)}) %collective-permute-start.10) | collective-permute-done | bytes 131104 | tf_op jit(solution)/shard_map/ppermute | solution.py:378
  94.6 1.9 %collective-permute-start.11 = (f32[2,16,512]{2,1,0:T(8,128)S(1)}, f32[2,16,512]{2,1,0:T(8,128)S(1)}, u32[]{:S(2)}, u32[]{:S(2)}) collective-permute-start(f32[2,16,512]{2,1,0:T(8,128)S(1)} %dynamic-slice_bitcast_fusion.1), channel_id=1, source_target_pairs={{0,2},{1,3},{2,0},{3,1},{4,6},{5,7},{6,4},{7,5},{8,10},{9,11},{10,... | collective-permute-start | bytes 196616 | tf_op jit(solution)/shard_map/ppermute | solution.py:378
  96.5 4.2 %collective-permute-done.11 = f32[2,16,512]{2,1,0:T(8,128)S(1)} collective-permute-done((f32[2,16,512]{2,1,0:T(8,128)S(1)}, f32[2,16,512]{2,1,0:T(8,128)S(1)}, u32[]{:S(2)}, u32[]{:S(2)}) %collective-permute-start.11) | collective-permute-done | bytes 65568 | tf_op jit(solution)/shard_map/ppermute | solution.py:378
  (41 shorter events, 9.2 us)
Async XLA Ops:
  0.0 11.7 %collective-permute-start = (f32[2,128,512]{2,1,0:T(8,128)}, f32[2,128,512]{2,1,0:T(8,128)S(1)}, u32[]{:S(2)}, u32[]{:S(2)}) collective-permute-start(f32[2,128,512]{2,1,0:T(8,128)} %own_ref.1), channel_id=1, source_target_pairs={{0,8},{2,10},{4,12},{6,14},{8,16},{9,1},{10,18},{11,3},{12,20},{13... | collective-permute-start | bytes 1572872 | tf_op jit(solution)/shard_map/ppermute | solution.py:339
  4.7 13.5 %collective-permute-start.2 = (f32[2,256,256]{2,1,0:T(8,128)}, f32[2,256,256]{2,1,0:T(8,128)S(1)}, u32[]{:S(2)}, u32[]{:S(2)}) collective-permute-start(f32[2,256,256]{2,1,0:T(8,128)} %bitcast.35), channel_id=1, source_target_pairs={{0,1},{1,0},{2,3},{3,2},{4,5},{5,4},{6,7},{7,6},{8,9},{9,8},{10,11... | collective-permute-start | bytes 1572872 | tf_op jit(solution)/shard_map/ppermute | solution.py:340
  11.7 6.5 %copy-start.8 = (f32[2,128,512]{2,1,0:T(8,128)}, f32[2,128,512]{2,1,0:T(8,128)S(1)}, u32[]{:S(2)}) copy-start(f32[2,128,512]{2,1,0:T(8,128)S(1)} %collective-permute-done.before_ref) | copy-start | bytes 1572868
  11.7 6.5 %collective-permute-start.1 = (f32[2,128,512]{2,1,0:T(8,128)S(1)}, f32[2,128,512]{2,1,0:T(8,128)S(1)}, u32[]{:S(2)}, u32[]{:S(2)}) collective-permute-start(f32[2,128,512]{2,1,0:T(8,128)S(1)} %collective-permute-done.before_ref), channel_id=1, source_target_pairs={{0,1},{1,0},{2,3},{3,2},{4,5},{5,4},{6,7},{7,6},{8,9},{9,8},{10,11... | collective-permute-start | bytes 1572872 | tf_op jit(solution)/shard_map/ppermute | solution.py:341
  18.2 0.8 copy-start.4
  18.2 1.0 copy-start.9
  24.8 10.1 %collective-permute-start.5 = (f32[256,256]{1,0:T(8,128)}, f32[256,256]{1,0:T(8,128)S(1)}, u32[]{:S(2)}, u32[]{:S(2)}) collective-permute-start(f32[256,256]{1,0:T(8,128)} %get-tuple-element.15), channel_id=1, source_target_pairs={{0,6},{1,7},{2,4},{3,5},{4,2},{5,3},{6,0},{7,1},{8,14},{9,15},{10,... | collective-permute-start | bytes 786440 | tf_op jit(solution)/shard_map/ppermute | solution.py:40
  29.5 8.9 %copy-start.6 = (f32[256,256]{1,0:T(8,128)S(1)}, f32[256,256]{1,0:T(8,128)}, u32[]{:S(2)}) copy-start(f32[256,256]{1,0:T(8,128)} %get-tuple-element.14) | copy-start | bytes 786436
  29.5 8.9 %collective-permute-start.3 = (f32[256,256]{1,0:T(8,128)}, f32[256,256]{1,0:T(8,128)S(1)}, u32[]{:S(2)}, u32[]{:S(2)}) collective-permute-start(f32[256,256]{1,0:T(8,128)} %get-tuple-element.14), channel_id=1, source_target_pairs={{0,2},{1,3},{2,0},{3,1},{4,6},{5,7},{6,4},{7,5},{8,10},{9,11},{10,... | collective-permute-start | bytes 786440 | tf_op jit(solution)/shard_map/ppermute | solution.py:39
  35.9 2.5 %copy-start = (f32[256,256]{1,0:T(8,128)}, f32[256,256]{1,0:T(8,128)S(1)}, u32[]{:S(2)}) copy-start(f32[256,256]{1,0:T(8,128)S(1)} %add.90.mb_ref) | copy-start | bytes 786436
  35.9 8.3 %collective-permute-start.6 = (f32[256,256]{1,0:T(8,128)S(1)}, f32[256,256]{1,0:T(8,128)S(1)}, u32[]{:S(2)}, u32[]{:S(2)}) collective-permute-start(f32[256,256]{1,0:T(8,128)S(1)} %add.90.mb_ref), channel_id=1, source_target_pairs={{0,2},{1,3},{2,0},{3,1},{4,6},{5,7},{6,4},{7,5},{8,10},{9,11},{10,... | collective-permute-start | bytes 786440 | tf_op jit(solution)/shard_map/ppermute | solution.py:41
  38.4 9.5 %copy-start.1 = (f32[256,256]{1,0:T(8,128)}, f32[256,256]{1,0:T(8,128)S(1)}, u32[]{:S(2)}) copy-start(f32[256,256]{1,0:T(8,128)S(1)} %add.89.ma_ref) | copy-start | bytes 786436
  38.4 9.5 %collective-permute-start.4 = (f32[256,256]{1,0:T(8,128)S(1)}, f32[256,256]{1,0:T(8,128)S(1)}, u32[]{:S(2)}, u32[]{:S(2)}) collective-permute-start(f32[256,256]{1,0:T(8,128)S(1)} %add.89.ma_ref), channel_id=1, source_target_pairs={{0,6},{1,7},{2,4},{3,5},{4,2},{5,3},{6,0},{7,1},{8,14},{9,15},{10,... | collective-permute-start | bytes 786440 | tf_op jit(solution)/shard_map/ppermute | solution.py:41
  44.1 3.8 %copy-start.5 = (f32[256,256]{1,0:T(8,128)}, f32[256,256]{1,0:T(8,128)S(1)}, u32[]{:S(2)}) copy-start(f32[256,256]{1,0:T(8,128)S(1)} %collective-permute-done.6.rb_ref) | copy-start | bytes 786436
  47.9 0.7 copy-start.7
  55.4 4.5 %collective-permute-start.7 = (f32[432,512]{1,0:T(8,128)}, f32[432,512]{1,0:T(8,128)S(1)}, u32[]{:S(2)}, u32[]{:S(2)}) collective-permute-start(f32[432,512]{1,0:T(8,128)} %get-tuple-element.17), channel_id=1, source_target_pairs={{0,1},{1,0},{2,3},{3,2},{4,5},{5,4},{6,7},{7,6},{8,9},{9,8},{10,11... | collective-permute-start | bytes 2654216 | tf_op jit(solution)/shard_map/ppermute | solution.py:358
  62.2 15.6 %collective-permute-start.8 = (f32[144,512]{1,0:T(8,128)S(1)}, f32[144,512]{1,0:T(8,128)S(1)}, u32[]{:S(2)}, u32[]{:S(2)}) collective-permute-start(f32[144,512]{1,0:T(8,128)S(1)} %pad_maximum_fusion), channel_id=1, source_target_pairs={{0,8},{8,16},{16,24},{24,32},{32,40},{40,48},{48,56},{56,64},{64,7... | collective-permute-start | bytes 884744 | tf_op jit(solution)/shard_map/ppermute | solution.py:366
  71.3 14.0 %collective-permute-start.9 = (f32[144,512]{1,0:T(8,128)S(1)}, f32[144,512]{1,0:T(8,128)S(1)}, u32[]{:S(2)}, u32[]{:S(2)}) collective-permute-start(f32[144,512]{1,0:T(8,128)S(1)} %pad_maximum_fusion.1), channel_id=1, source_target_pairs={{8,0},{16,8},{24,16},{32,24},{40,32},{48,40},{56,48},{64,56},{72,6... | collective-permute-start | bytes 884744 | tf_op jit(solution)/shard_map/ppermute | solution.py:367
  77.8 0.7 copy-start.2
  85.3 1.0 slice-start
  86.3 10.2 %copy-start.3 = (f32[144,512]{1,0:T(8,128)S(1)}, f32[144,512]{1,0:T(8,128)}, u32[]{:S(2)}) copy-start(f32[144,512]{1,0:T(8,128)} %copy-done.2) | copy-start | bytes 884740
  86.3 8.2 %collective-permute-start.10 = (f32[2,2,16,512]{3,2,1,0:T(8,128)S(1)}, f32[2,2,16,512]{3,2,1,0:T(8,128)S(1)}, u32[]{:S(2)}, u32[]{:S(2)}) collective-permute-start(f32[2,2,16,512]{3,2,1,0:T(8,128)S(1)} %dynamic-slice_bitcast_fusion), channel_id=1, source_target_pairs={{0,6},{1,7},{2,4},{3,5},{4,2},{5,3},{6,0},{7,1},{8,14},{9,15},{10,... | collective-permute-start | bytes 393224 | tf_op jit(solution)/shard_map/ppermute | solution.py:378
  94.6 6.2 %collective-permute-start.11 = (f32[2,16,512]{2,1,0:T(8,128)S(1)}, f32[2,16,512]{2,1,0:T(8,128)S(1)}, u32[]{:S(2)}, u32[]{:S(2)}) collective-permute-start(f32[2,16,512]{2,1,0:T(8,128)S(1)} %dynamic-slice_bitcast_fusion.1), channel_id=1, source_target_pairs={{0,2},{1,3},{2,0},{3,1},{4,6},{5,7},{6,4},{7,5},{8,10},{9,11},{10,... | collective-permute-start | bytes 196616 | tf_op jit(solution)/shard_map/ppermute | solution.py:378
where the time goes:
time: 103 us; the launch traced here: 102 us
  starting transfers between devices  42.9 us (42%)
  waiting for transfers between devices  35.3 us (34%)
  Pallas kernels  12.4 us (12%)
  other arithmetic  7.17 us (7%)
  local copies, waits for them, and re-layouts  3.47 us (3%)
    ppermute x1, starting transfers between devices, local(): from_prev = lax.ppermute(to_next, 'pos', neighbour_pairs(pos_count, 1))  9.06 us
    ppermute x2, waiting for transfers between devices, local(): tile = keep + lax.ppermute(send, 'mode', pairs)  7.61 us
    pallas_call x1, Pallas kernels, run_backward(): pl.pallas_call(backward_kernel, grid_spec=pltpu.PrefetchScalarGridSpec(nu...  6.8 us
    ppermute x1, waiting for transfers between devices, local(): from_next = lax.ppermute(to_prev, 'pos', neighbour_pairs(pos_count, -1))  6.74 us
    ppermute x2, starting transfers between devices, local(): tile = keep + lax.ppermute(send, 'mode', pairs)  6.66 us
    pallas_call x1, Pallas kernels, run_forward(): pl.pallas_call(forward_kernel, grid_spec=pltpu.PrefetchScalarGridSpec(num...  5.58 us
    ppermute x1, waiting for transfers between devices, local(): fetched = lax.ppermute(object_field, ('pos', 'mode'), halo_pairs)  5.06 us
    ppermute x1, starting transfers between devices, local(): fetched = lax.ppermute(object_field, ('pos', 'mode'), halo_pairs)  4.69 us
  transfers between devices with their start and end apart: 12, of which 10 were waited for; matrix products, arithmetic and copies ran while one was open for 3% of the time, Pallas kernels for 0%

commit v1 on v0

--- a/solution.py
+++ b/solution.py
@@ -1,6 +1,8 @@
 import math
 
 import jax
+import ml_dtypes
+import numpy as np
 import jax.numpy as jnp
 from jax import lax
 from jax.experimental import pallas as pl
@@ -9,14 +11,13 @@
 
 
 def dft_tables(pattern):
-    counter = jnp.arange(pattern, dtype=jnp.int32)
+    counter = np.arange(pattern, dtype=np.int32)
     phases = counter[:, None] * counter[None, :] % pattern
-    angles = phases.astype(jnp.float32) * (2.0 * math.pi / pattern)
-    factor = 1.0 / math.sqrt(pattern)
-    return (
-        (jnp.cos(angles) * factor).astype(jnp.bfloat16),
-        (-jnp.sin(angles) * factor).astype(jnp.bfloat16),
-    )
+    angles = phases.astype(np.float32) * np.float32(2.0 * math.pi / pattern)
+    factor = np.float32(1.0 / math.sqrt(pattern))
+    real = (np.cos(angles) * factor).astype(np.float32).astype(ml_dtypes.bfloat16)
+    imag = (-np.sin(angles) * factor).astype(np.float32).astype(ml_dtypes.bfloat16)
+    return jnp.asarray(real), jnp.asarray(imag)
 
 
 def neighbour_pairs(size, step):

time: 103 us -> 101 us (0.981); the launches traced: 102 us -> 102 us
  other arithmetic: 7.17 us -> 5.48 us
    convert_element_type x1 -> x0, other arithmetic: 1.76 us -> none  [dft_tables(): (-jnp.sin(angles) * factor).astype(jnp.bfloat16)]
    ppermute x1, starting transfers between devices: 9.06 us -> 10.2 us  [local(): from_prev = lax.ppermute(to_next, 'pos', neighbour_pairs(pos_count, 1))]
  transfers between devices with their start and end apart: 12 -> 12, of which waited for: 10 -> 11; matrix products, arithmetic and copies ran while one was open for 3% -> 2% of each run, Pallas kernels for 0% -> 0%
where the time goes in v1:
time: 101 us; the launch traced here: 102 us
  starting transfers between devices  43.9 us (43%)
  waiting for transfers between devices  35.6 us (35%)
  Pallas kernels  12.3 us (12%)
  other arithmetic  5.48 us (5%)
  local copies, waits for them, and re-layouts  3.87 us (4%)
    ppermute x1, starting transfers between devices, local(): from_prev = lax.ppermute(to_next, 'pos', neighbour_pairs(pos_count, 1))  10.2 us
    ppermute x2, waiting for transfers between devices, local(): tile = keep + lax.ppermute(send, 'mode', pairs)  7.75 us
    pallas_call x1, Pallas kernels, run_backward(): pl.pallas_call(backward_kernel, grid_spec=pltpu.PrefetchScalarGridSpec(nu...  6.78 us
    ppermute x1, waiting for transfers between devices, local(): from_next = lax.ppermute(to_prev, 'pos', neighbour_pairs(pos_count, -1))  6.76 us
    ppermute x2, starting transfers between devices, local(): tile = keep + lax.ppermute(send, 'mode', pairs)  6.53 us
    pallas_call x1, Pallas kernels, run_forward(): pl.pallas_call(forward_kernel, grid_spec=pltpu.PrefetchScalarGridSpec(num...  5.54 us
    ppermute x1, waiting for transfers between devices, local(): fetched = lax.ppermute(object_field, ('pos', 'mode'), halo_pairs)  5.06 us
    ppermute x1, starting transfers between devices, local(): fetched = lax.ppermute(object_field, ('pos', 'mode'), halo_pairs)  4.69 us
  transfers between devices with their start and end apart: 12, of which 11 were waited for; matrix products, arithmetic and copies ran while one was open for 2% of the time, Pallas kernels for 0%

profile of v1, /device:TPU:248, one launch (start us, length us, event | category | flops | bytes accessed | tf_op | source)
XLA Modules:
  0.0 102.2 jit_solution(18002985773804478121)
XLA Ops:
  0.0 4.7 %collective-permute-start = (f32[2,128,512]{2,1,0:T(8,128)}, f32[2,128,512]{2,1,0:T(8,128)S(1)}, u32[]{:S(2)}, u32[]{:S(2)}) collective-permute-start(f32[2,128,512]{2,1,0:T(8,128)} %own_ref.1), channel_id=1, source_target_pairs={{0,8},{2,10},{4,12},{6,14},{8,16},{9,1},{10,18},{11,3},{12,20},{13... | collective-permute-start | bytes 1572872 | tf_op jit(solution)/shard_map/ppermute | solution.py:340
  4.7 1.9 %collective-permute-start.2 = (f32[2,256,256]{2,1,0:T(8,128)}, f32[2,256,256]{2,1,0:T(8,128)S(1)}, u32[]{:S(2)}, u32[]{:S(2)}) collective-permute-start(f32[2,256,256]{2,1,0:T(8,128)} %bitcast.35), channel_id=1, source_target_pairs={{0,1},{1,0},{2,3},{3,2},{4,5},{5,4},{6,7},{7,6},{8,9},{9,8},{10,11... | collective-permute-start | bytes 1572872 | tf_op jit(solution)/shard_map/ppermute | solution.py:341
  6.6 5.1 %collective-permute-done.before_ref = f32[2,128,512]{2,1,0:T(8,128)S(1)} collective-permute-done((f32[2,128,512]{2,1,0:T(8,128)}, f32[2,128,512]{2,1,0:T(8,128)S(1)}, u32[]{:S(2)}, u32[]{:S(2)}) %collective-permute-start) | collective-permute-done | bytes 524320 | tf_op jit(solution)/shard_map/ppermute | solution.py:340
  11.7 3.5 %collective-permute-start.1 = (f32[2,128,512]{2,1,0:T(8,128)S(1)}, f32[2,128,512]{2,1,0:T(8,128)S(1)}, u32[]{:S(2)}, u32[]{:S(2)}) collective-permute-start(f32[2,128,512]{2,1,0:T(8,128)S(1)} %collective-permute-done.before_ref), channel_id=1, source_target_pairs={{0,1},{1,0},{2,3},{3,2},{4,5},{5,4},{6,7},{7,6},{8,9},{9,8},{10,11... | collective-permute-start | bytes 1572872 | tf_op jit(solution)/shard_map/ppermute | solution.py:342
  18.1 5.5 %shard_map.82 = (bf16[2,2,2,256,256]{4,3,2,1,0:T(8,128)(2,1)}, bf16[2,2,2,256,256]{4,3,2,1,0:T(8,128)(2,1)}, f32[256,256]{1,0:T(8,128)}, f32[256,256]{1,0:T(8,128)}) custom-call(s32[3]{0:T(128)} %roff.3, s32[3]{0:T(128)} %coff.3, s32[1]{0:T(128)S(6)} %copy.27.cnt, s32[2]{0:T(128)} %pad_add_fusion.core, f32[2,128,512]{2,1,0:T(8,128)} %copy-done.8, ...), custom_call_target="tpu_custom_call" | custom-call | flops 1073741824 | bytes 10485760 | tf_op jit(solution)/shard_map/pallas_call | solution.py:237
  23.6 4.7 %collective-permute-start.5 = (f32[256,256]{1,0:T(8,128)}, f32[256,256]{1,0:T(8,128)S(1)}, u32[]{:S(2)}, u32[]{:S(2)}) collective-permute-start(f32[256,256]{1,0:T(8,128)} %get-tuple-element.15), channel_id=1, source_target_pairs={{0,6},{1,7},{2,4},{3,5},{4,2},{5,3},{6,0},{7,1},{8,14},{9,15},{10,... | collective-permute-start | bytes 786440 | tf_op jit(solution)/shard_map/ppermute | solution.py:41
  28.3 2.3 %collective-permute-start.3 = (f32[256,256]{1,0:T(8,128)}, f32[256,256]{1,0:T(8,128)S(1)}, u32[]{:S(2)}, u32[]{:S(2)}) collective-permute-start(f32[256,256]{1,0:T(8,128)} %get-tuple-element.14), channel_id=1, source_target_pairs={{0,2},{1,3},{2,0},{3,1},{4,6},{5,7},{6,4},{7,5},{8,10},{9,11},{10,... | collective-permute-start | bytes 786440 | tf_op jit(solution)/shard_map/ppermute | solution.py:40
  30.6 3.1 %collective-permute-done.5 = f32[256,256]{1,0:T(8,128)S(1)} collective-permute-done((f32[256,256]{1,0:T(8,128)}, f32[256,256]{1,0:T(8,128)S(1)}, u32[]{:S(2)}, u32[]{:S(2)}) %collective-permute-start.5) | collective-permute-done | bytes 262176 | tf_op jit(solution)/shard_map/ppermute | solution.py:41
  34.7 2.2 %collective-permute-start.6 = (f32[256,256]{1,0:T(8,128)S(1)}, f32[256,256]{1,0:T(8,128)S(1)}, u32[]{:S(2)}, u32[]{:S(2)}) collective-permute-start(f32[256,256]{1,0:T(8,128)S(1)} %add.77.mb_ref), channel_id=1, source_target_pairs={{0,2},{1,3},{2,0},{3,1},{4,6},{5,7},{6,4},{7,5},{8,10},{9,11},{10,... | collective-permute-start | bytes 786440 | tf_op jit(solution)/shard_map/ppermute | solution.py:42
  37.3 4.1 %collective-permute-start.4 = (f32[256,256]{1,0:T(8,128)S(1)}, f32[256,256]{1,0:T(8,128)S(1)}, u32[]{:S(2)}, u32[]{:S(2)}) collective-permute-start(f32[256,256]{1,0:T(8,128)S(1)} %add.76.ma_ref), channel_id=1, source_target_pairs={{0,6},{1,7},{2,4},{3,5},{4,2},{5,3},{6,0},{7,1},{8,14},{9,15},{10,... | collective-permute-start | bytes 786440 | tf_op jit(solution)/shard_map/ppermute | solution.py:42
  41.4 1.6 %collective-permute-done.6.rb_ref = f32[256,256]{1,0:T(8,128)S(1)} collective-permute-done((f32[256,256]{1,0:T(8,128)S(1)}, f32[256,256]{1,0:T(8,128)S(1)}, u32[]{:S(2)}, u32[]{:S(2)}) %collective-permute-start.6) | collective-permute-done | bytes 262176 | tf_op jit(solution)/shard_map/ppermute | solution.py:42
  43.0 3.7 %collective-permute-done.4.ra_ref = f32[256,256]{1,0:T(8,128)S(1)} collective-permute-done((f32[256,256]{1,0:T(8,128)S(1)}, f32[256,256]{1,0:T(8,128)S(1)}, u32[]{:S(2)}, u32[]{:S(2)}) %collective-permute-start.4) | collective-permute-done | bytes 262176 | tf_op jit(solution)/shard_map/ppermute | solution.py:42
  47.4 6.8 %shard_map.83 = (f32[384,512]{1,0:T(8,128)}, f32[432,512]{1,0:T(8,128)}, f32[48,512]{1,0:T(8,128)}) custom-call(s32[3]{0:T(128)} %roff.3, s32[3]{0:T(128)} %coff.3, s32[1]{0:T(128)S(6)} %copy.27.cnt, s32[2]{0:T(128)} %pad_add_fusion.core, bf16[2,2,2,256,256]{4,3,2,1,0:T(8,128)(2,1)} %get-tuple-element.12.exit_ref, ...), custom_call_target="tpu_custom_call" | custom-call | flops 1073741824 | bytes 12582912 | tf_op jit(solution)/shard_map/pallas_call | solution.py:282
  54.2 1.9 %collective-permute-start.7 = (f32[432,512]{1,0:T(8,128)}, f32[432,512]{1,0:T(8,128)S(1)}, u32[]{:S(2)}, u32[]{:S(2)}) collective-permute-start(f32[432,512]{1,0:T(8,128)} %get-tuple-element.17), channel_id=1, source_target_pairs={{0,1},{1,0},{2,3},{3,2},{4,5},{5,4},{6,7},{7,6},{8,9},{9,8},{10,11... | collective-permute-start | bytes 2654216 | tf_op jit(solution)/shard_map/ppermute | solution.py:359
  56.1 2.6 %collective-permute-done.7 = f32[432,512]{1,0:T(8,128)S(1)} collective-permute-done((f32[432,512]{1,0:T(8,128)}, f32[432,512]{1,0:T(8,128)S(1)}, u32[]{:S(2)}, u32[]{:S(2)}) %collective-permute-start.7) | collective-permute-done | bytes 884768 | tf_op jit(solution)/shard_map/ppermute | solution.py:359
  61.0 10.2 %collective-permute-start.8 = (f32[144,512]{1,0:T(8,128)S(1)}, f32[144,512]{1,0:T(8,128)S(1)}, u32[]{:S(2)}, u32[]{:S(2)}) collective-permute-start(f32[144,512]{1,0:T(8,128)S(1)} %pad_maximum_fusion), channel_id=1, source_target_pairs={{0,8},{8,16},{16,24},{24,32},{32,40},{40,48},{48,56},{56,64},{64,7... | collective-permute-start | bytes 884744 | tf_op jit(solution)/shard_map/ppermute | solution.py:367
  71.3 1.9 %collective-permute-start.9 = (f32[144,512]{1,0:T(8,128)S(1)}, f32[144,512]{1,0:T(8,128)S(1)}, u32[]{:S(2)}, u32[]{:S(2)}) collective-permute-start(f32[144,512]{1,0:T(8,128)S(1)} %pad_maximum_fusion.1), channel_id=1, source_target_pairs={{8,0},{16,8},{24,16},{32,24},{40,32},{48,40},{56,48},{64,56},{72,6... | collective-permute-start | bytes 884744 | tf_op jit(solution)/shard_map/ppermute | solution.py:368
  73.2 4.6 %collective-permute-done.8 = f32[144,512]{1,0:T(8,128)S(1)} collective-permute-done((f32[144,512]{1,0:T(8,128)S(1)}, f32[144,512]{1,0:T(8,128)S(1)}, u32[]{:S(2)}, u32[]{:S(2)}) %collective-permute-start.8) | collective-permute-done | bytes 294944 | tf_op jit(solution)/shard_map/ppermute | solution.py:367
  78.5 6.8 %collective-permute-done.9 = f32[144,512]{1,0:T(8,128)S(1)} collective-permute-done((f32[144,512]{1,0:T(8,128)S(1)}, f32[144,512]{1,0:T(8,128)S(1)}, u32[]{:S(2)}, u32[]{:S(2)}) %collective-permute-start.9) | collective-permute-done | bytes 294944 | tf_op jit(solution)/shard_map/ppermute | solution.py:368
  86.3 4.6 %collective-permute-start.10 = (f32[2,2,16,512]{3,2,1,0:T(8,128)S(1)}, f32[2,2,16,512]{3,2,1,0:T(8,128)S(1)}, u32[]{:S(2)}, u32[]{:S(2)}) collective-permute-start(f32[2,2,16,512]{3,2,1,0:T(8,128)S(1)} %dynamic-slice_bitcast_fusion), channel_id=1, source_target_pairs={{0,6},{1,7},{2,4},{3,5},{4,2},{5,3},{6,0},{7,1},{8,14},{9,15},{10,... | collective-permute-start | bytes 393224 | tf_op jit(solution)/shard_map/ppermute | solution.py:379
  91.0 3.5 %collective-permute-done.10 = f32[2,2,16,512]{3,2,1,0:T(8,128)S(1)} collective-permute-done((f32[2,2,16,512]{3,2,1,0:T(8,128)S(1)}, f32[2,2,16,512]{3,2,1,0:T(8,128)S(1)}, u32[]{:S(2)}, u32[]{:S(2)}) %collective-permute-start.10) | collective-permute-done | bytes 131104 | tf_op jit(solution)/shard_map/ppermute | solution.py:379
  94.5 1.9 %collective-permute-start.11 = (f32[2,16,512]{2,1,0:T(8,128)S(1)}, f32[2,16,512]{2,1,0:T(8,128)S(1)}, u32[]{:S(2)}, u32[]{:S(2)}) collective-permute-start(f32[2,16,512]{2,1,0:T(8,128)S(1)} %dynamic-slice_bitcast_fusion.1), channel_id=1, source_target_pairs={{0,2},{1,3},{2,0},{3,1},{4,6},{5,7},{6,4},{7,5},{8,10},{9,11},{10,... | collective-permute-start | bytes 196616 | tf_op jit(solution)/shard_map/ppermute | solution.py:379
  96.5 4.2 %collective-permute-done.11 = f32[2,16,512]{2,1,0:T(8,128)S(1)} collective-permute-done((f32[2,16,512]{2,1,0:T(8,128)S(1)}, f32[2,16,512]{2,1,0:T(8,128)S(1)}, u32[]{:S(2)}, u32[]{:S(2)}) %collective-permute-start.11) | collective-permute-done | bytes 65568 | tf_op jit(solution)/shard_map/ppermute | solution.py:379
  100.7 1.5 %fusion.3 = f32[2,16,512]{2,1,0:T(8,128)} fusion(f32[2,16,512]{2,1,0:T(8,128)S(1)} %collective-permute-done.11, f32[2,2,16,512]{3,2,1,0:T(8,128)S(1)} %bitcast_add_fusion, s32[]{:T(128)S(6)} %select_n.47, f32[2,128,512]{2,1,0:T(8,128)} %own_ref.1, s32[]{:T(128)S(6)} %select_n.39, f32[16,512]{1,0:T(8,128)S(1)} %fusion.4), kind=kLoop, calls=%fused_computation.11 | loop fusion | flops 49152 | bytes 294920 | tf_op jit(solution)/shard_map/add | solution.py:383
  (40 shorter events, 8.3 us)
Async XLA Ops:
  0.0 11.7 %collective-permute-start = (f32[2,128,512]{2,1,0:T(8,128)}, f32[2,128,512]{2,1,0:T(8,128)S(1)}, u32[]{:S(2)}, u32[]{:S(2)}) collective-permute-start(f32[2,128,512]{2,1,0:T(8,128)} %own_ref.1), channel_id=1, source_target_pairs={{0,8},{2,10},{4,12},{6,14},{8,16},{9,1},{10,18},{11,3},{12,20},{13... | collective-permute-start | bytes 1572872 | tf_op jit(solution)/shard_map/ppermute | solution.py:340
  4.7 11.8 %collective-permute-start.2 = (f32[2,256,256]{2,1,0:T(8,128)}, f32[2,256,256]{2,1,0:T(8,128)S(1)}, u32[]{:S(2)}, u32[]{:S(2)}) collective-permute-start(f32[2,256,256]{2,1,0:T(8,128)} %bitcast.35), channel_id=1, source_target_pairs={{0,1},{1,0},{2,3},{3,2},{4,5},{5,4},{6,7},{7,6},{8,9},{9,8},{10,11... | collective-permute-start | bytes 1572872 | tf_op jit(solution)/shard_map/ppermute | solution.py:341
  11.7 5.0 %copy-start.8 = (f32[2,128,512]{2,1,0:T(8,128)}, f32[2,128,512]{2,1,0:T(8,128)S(1)}, u32[]{:S(2)}) copy-start(f32[2,128,512]{2,1,0:T(8,128)S(1)} %collective-permute-done.before_ref) | copy-start | bytes 1572868
  11.7 5.0 %collective-permute-start.1 = (f32[2,128,512]{2,1,0:T(8,128)S(1)}, f32[2,128,512]{2,1,0:T(8,128)S(1)}, u32[]{:S(2)}, u32[]{:S(2)}) collective-permute-start(f32[2,128,512]{2,1,0:T(8,128)S(1)} %collective-permute-done.before_ref), channel_id=1, source_target_pairs={{0,1},{1,0},{2,3},{3,2},{4,5},{5,4},{6,7},{7,6},{8,9},{9,8},{10,11... | collective-permute-start | bytes 1572872 | tf_op jit(solution)/shard_map/ppermute | solution.py:342
  16.5 0.8 copy-start.4
  17.3 0.8 copy-start.9
  23.6 10.1 %collective-permute-start.5 = (f32[256,256]{1,0:T(8,128)}, f32[256,256]{1,0:T(8,128)S(1)}, u32[]{:S(2)}, u32[]{:S(2)}) collective-permute-start(f32[256,256]{1,0:T(8,128)} %get-tuple-element.15), channel_id=1, source_target_pairs={{0,6},{1,7},{2,4},{3,5},{4,2},{5,3},{6,0},{7,1},{8,14},{9,15},{10,... | collective-permute-start | bytes 786440 | tf_op jit(solution)/shard_map/ppermute | solution.py:41
  28.3 8.9 %copy-start.6 = (f32[256,256]{1,0:T(8,128)S(1)}, f32[256,256]{1,0:T(8,128)}, u32[]{:S(2)}) copy-start(f32[256,256]{1,0:T(8,128)} %get-tuple-element.14) | copy-start | bytes 786436
  28.3 8.9 %collective-permute-start.3 = (f32[256,256]{1,0:T(8,128)}, f32[256,256]{1,0:T(8,128)S(1)}, u32[]{:S(2)}, u32[]{:S(2)}) collective-permute-start(f32[256,256]{1,0:T(8,128)} %get-tuple-element.14), channel_id=1, source_target_pairs={{0,2},{1,3},{2,0},{3,1},{4,6},{5,7},{6,4},{7,5},{8,10},{9,11},{10,... | collective-permute-start | bytes 786440 | tf_op jit(solution)/shard_map/ppermute | solution.py:40
  34.7 2.5 %copy-start = (f32[256,256]{1,0:T(8,128)}, f32[256,256]{1,0:T(8,128)S(1)}, u32[]{:S(2)}) copy-start(f32[256,256]{1,0:T(8,128)S(1)} %add.77.mb_ref) | copy-start | bytes 786436
  34.7 8.3 %collective-permute-start.6 = (f32[256,256]{1,0:T(8,128)S(1)}, f32[256,256]{1,0:T(8,128)S(1)}, u32[]{:S(2)}, u32[]{:S(2)}) collective-permute-start(f32[256,256]{1,0:T(8,128)S(1)} %add.77.mb_ref), channel_id=1, source_target_pairs={{0,2},{1,3},{2,0},{3,1},{4,6},{5,7},{6,4},{7,5},{8,10},{9,11},{10,... | collective-permute-start | bytes 786440 | tf_op jit(solution)/shard_map/ppermute | solution.py:42
  37.2 9.5 %copy-start.1 = (f32[256,256]{1,0:T(8,128)}, f32[256,256]{1,0:T(8,128)S(1)}, u32[]{:S(2)}) copy-start(f32[256,256]{1,0:T(8,128)S(1)} %add.76.ma_ref) | copy-start | bytes 786436
  37.3 9.5 %collective-permute-start.4 = (f32[256,256]{1,0:T(8,128)S(1)}, f32[256,256]{1,0:T(8,128)S(1)}, u32[]{:S(2)}, u32[]{:S(2)}) collective-permute-start(f32[256,256]{1,0:T(8,128)S(1)} %add.76.ma_ref), channel_id=1, source_target_pairs={{0,6},{1,7},{2,4},{3,5},{4,2},{5,3},{6,0},{7,1},{8,14},{9,15},{10,... | collective-permute-start | bytes 786440 | tf_op jit(solution)/shard_map/ppermute | solution.py:42
  43.0 3.8 %copy-start.5 = (f32[256,256]{1,0:T(8,128)}, f32[256,256]{1,0:T(8,128)S(1)}, u32[]{:S(2)}) copy-start(f32[256,256]{1,0:T(8,128)S(1)} %collective-permute-done.6.rb_ref) | copy-start | bytes 786436
  46.7 0.7 copy-start.7
  54.2 4.5 %collective-permute-start.7 = (f32[432,512]{1,0:T(8,128)}, f32[432,512]{1,0:T(8,128)S(1)}, u32[]{:S(2)}, u32[]{:S(2)}) collective-permute-start(f32[432,512]{1,0:T(8,128)} %get-tuple-element.17), channel_id=1, source_target_pairs={{0,1},{1,0},{2,3},{3,2},{4,5},{5,4},{6,7},{7,6},{8,9},{9,8},{10,11... | collective-permute-start | bytes 2654216 | tf_op jit(solution)/shard_map/ppermute | solution.py:359
  61.0 16.7 %collective-permute-start.8 = (f32[144,512]{1,0:T(8,128)S(1)}, f32[144,512]{1,0:T(8,128)S(1)}, u32[]{:S(2)}, u32[]{:S(2)}) collective-permute-start(f32[144,512]{1,0:T(8,128)S(1)} %pad_maximum_fusion), channel_id=1, source_target_pairs={{0,8},{8,16},{16,24},{24,32},{32,40},{40,48},{48,56},{56,64},{64,7... | collective-permute-start | bytes 884744 | tf_op jit(solution)/shard_map/ppermute | solution.py:367
  71.3 14.0 %collective-permute-start.9 = (f32[144,512]{1,0:T(8,128)S(1)}, f32[144,512]{1,0:T(8,128)S(1)}, u32[]{:S(2)}, u32[]{:S(2)}) collective-permute-start(f32[144,512]{1,0:T(8,128)S(1)} %pad_maximum_fusion.1), channel_id=1, source_target_pairs={{8,0},{16,8},{24,16},{32,24},{40,32},{48,40},{56,48},{64,56},{72,6... | collective-permute-start | bytes 884744 | tf_op jit(solution)/shard_map/ppermute | solution.py:368
  77.8 0.7 copy-start.2
  85.2 1.0 slice-start
  86.3 10.2 %copy-start.3 = (f32[144,512]{1,0:T(8,128)S(1)}, f32[144,512]{1,0:T(8,128)}, u32[]{:S(2)}) copy-start(f32[144,512]{1,0:T(8,128)} %copy-done.2) | copy-start | bytes 884740
  86.3 8.2 %collective-permute-start.10 = (f32[2,2,16,512]{3,2,1,0:T(8,128)S(1)}, f32[2,2,16,512]{3,2,1,0:T(8,128)S(1)}, u32[]{:S(2)}, u32[]{:S(2)}) collective-permute-start(f32[2,2,16,512]{3,2,1,0:T(8,128)S(1)} %dynamic-slice_bitcast_fusion), channel_id=1, source_target_pairs={{0,6},{1,7},{2,4},{3,5},{4,2},{5,3},{6,0},{7,1},{8,14},{9,15},{10,... | collective-permute-start | bytes 393224 | tf_op jit(solution)/shard_map/ppermute | solution.py:379
  94.5 6.2 %collective-permute-start.11 = (f32[2,16,512]{2,1,0:T(8,128)S(1)}, f32[2,16,512]{2,1,0:T(8,128)S(1)}, u32[]{:S(2)}, u32[]{:S(2)}) collective-permute-start(f32[2,16,512]{2,1,0:T(8,128)S(1)} %dynamic-slice_bitcast_fusion.1), channel_id=1, source_target_pairs={{0,2},{1,3},{2,0},{3,1},{4,6},{5,7},{6,4},{7,5},{8,10},{9,11},{10,... | collective-permute-start | bytes 196616 | tf_op jit(solution)/shard_map/ppermute | solution.py:379
